TPU v7x, 32 devices: a whole 2x2x4 slice. The times are simulated.
32 devices in a mesh: parts: 2 (over y), tm: 4 (over z), chan: 2 (over x), sub: 2 (over core).
Axes of the slice: x: 2, y: 2, z: 4, core: 2. Of those that a mesh axis runs over, the one named last changes fastest.
Arguments:
- start_state: float32 [16, 2048], P(('parts', 'chan')), parts along dimension 0, may hold values from -6 to 6
- guess: bfloat16 [64, 8, 2048], P(('parts', 'tm', 'sub'), 'chan'), parts along dimension 0, may hold values from -6 to 6
- w_in: bfloat16 [576, 320], replicated, may hold values from -0.25 to 0.25
- w_mid: bfloat16 [2880, 320], replicated, may hold values from -0.109375 to 0.109375
- w_out: bfloat16 [2880, 64], replicated, may hold values from -0.875 to 0.875
- time_embed: bfloat16 [1000, 320], replicated, may hold values from -4 to 4
- levels: float32 [1000], replicated, may hold values from 0 to 70, as said below
- plan: int32 [130], P('parts'), parts along dimension 0, may hold values from 0 to 999, as said below
- offset: int32 [2], P('parts'), parts along dimension 0, may hold values from 0 to 32
Outputs:
- trajectory: float32 [64, 8, 2048], P(('parts', 'tm', 'sub'), 'chan'), parts along dimension 0
There are 2 independent parts, one for each index of `parts`. A program takes and returns all parts, laid end to end along the dimension named above; an argument that names none is the same for every part. Nothing has to cross between parts.
Inputs may be any that keep to these rules, and one draw needn't show every extreme that they name: `levels`: rises strictly with the timestep, by at most 0.07 from one timestep to the next. Strictly falling along the plan; the first entry is 999 and the last is 0.
All inputs are finite; a program needn't handle non-finite values.
Results may differ from a plain program's by a relative error of at most 0.003.
Values may be sent and summed in bfloat16 or wider, within the bound.
No kernel may reach another device: no remote copies, remote signals or barrier semaphores. Data moves between devices by JAX's collectives and lax.ppermute only.
A program may use at most 64 MiB of HBM per device.

v0:
```python
import jax
import jax.numpy as jnp
from jax import lax
from jax.sharding import PartitionSpec as P

ITERS = 2


def padded_2(block, sides, width):
    for axis, dim in sides:
        count = lax.axis_size(axis)
        forward = [(i, i + 1) for i in range(count - 1)]
        backward = [(target, source) for source, target in forward]
        low = lax.ppermute(
            lax.slice_in_dim(block, block.shape[dim] - width, None, axis=dim), axis, forward
        )
        high = lax.ppermute(lax.slice_in_dim(block, 0, width, axis=dim), axis, backward)
        block = jnp.concatenate([low, block, high], axis=dim)
    return block


def from_behind(array, axis, by):
    devices = lax.axis_size(axis)
    pairs = [(i, i + by) for i in range(devices) if 0 <= i + by < devices]
    return lax.ppermute(array, axis, pairs)


def carried_in(array, axis, combine, identity):
    devices, mine = (lax.axis_size(axis), lax.axis_index(axis))
    everything = lax.all_gather(array, axis)
    start = jnp.broadcast_to(jnp.asarray(identity, array.dtype), array.shape)

    def turn(k, before):
        reached = k < mine
        new = combine(before, everything[k])
        return jnp.where(reached, new, before)

    return lax.fori_loop(0, devices, turn, start)


def conv_valid(layer_in, weight):
    batch_size, rows_in, width_in, channels = layer_in.shape
    padded = jnp.pad(layer_in, ((0, 0), (0, 0), (1, 1), (0, 0)))
    rows_out = rows_in - 2
    patches = jnp.concatenate(
        [
            padded[:, row_off : row_off + rows_out, col_off : col_off + width_in, :]
            for row_off in range(3)
            for col_off in range(3)
        ],
        axis=-1,
    )
    product = jnp.dot(patches.reshape(-1, 9 * channels), weight, preferred_element_type=jnp.float32)
    return product.reshape(batch_size, rows_out, width_in, weight.shape[1])


def row_mask(values, first_row, total_rows):
    positions = first_row + jnp.arange(values.shape[1], dtype=jnp.int32)
    inside = (positions >= 0) & (positions < total_rows)
    return jnp.where(inside[None, :, None, None], values, 0.0)


def drift(layer_in, embed, w_in, w_mid, w_out):
    steps_dev, tile_rows, merged = layer_in.shape
    channels = w_out.shape[1]
    columns = merged // channels
    rimmed = padded_2(layer_in, (("chan", 1),), 3)
    first_row = lax.axis_index("chan") * tile_rows - 2
    total_rows = tile_rows * lax.axis_size("chan")
    first_act = (
        conv_valid(rimmed.reshape(steps_dev, tile_rows + 6, columns, channels), w_in)
        + embed[:, None, None, :]
    )
    first_hidden = row_mask(jax.nn.silu(first_act), first_row, total_rows).astype(jnp.bfloat16)
    second_act = jax.nn.silu(conv_valid(first_hidden, w_mid))
    second_hidden = row_mask(second_act, first_row + 1, total_rows).astype(jnp.bfloat16)
    drift_out = conv_valid(second_hidden, w_out)
    return drift_out.reshape(steps_dev, tile_rows, merged)


def shards(start_state, guess, w_in, w_mid, w_out, time_embed, levels, plan, offset):
    steps_dev = guess.shape[0]
    time_index = lax.axis_index(("tm", "sub"))
    first_step = time_index * steps_dev
    window_ids = lax.dynamic_slice_in_dim(plan, offset[0] + first_step, steps_dev + 1)
    one_hot = window_ids[:, None] == jnp.arange(levels.shape[0], dtype=jnp.int32)[None, :]
    noise = jnp.dot(one_hot.astype(jnp.float32), levels, precision=lax.Precision.HIGHEST)
    step_size = noise[1:] - noise[:-1]
    embed = jnp.dot(
        one_hot[:-1].astype(jnp.bfloat16), time_embed, preferred_element_type=jnp.float32
    )
    factor = jnp.where(first_step + jnp.arange(steps_dev, dtype=jnp.int32) == 0, 1.0, 1.5).astype(
        jnp.float32
    )
    layer_in = guess
    states_after = None
    for sweep in range(ITERS):
        drift_now = drift(layer_in, embed, w_in, w_mid, w_out)
        previous = from_behind(drift_now[-1], ("tm", "sub"), 1)
        earlier = jnp.concatenate([previous[None], drift_now[:-1]], axis=0)
        increment = step_size[:, None, None] * (factor[:, None, None] * drift_now - 0.5 * earlier)
        running = jnp.cumsum(increment, axis=0)
        device_total = running[-1]
        earlier_sum = carried_in(
            device_total,
            ("tm", "sub"),
            lambda before_sum, later_sum: before_sum + later_sum,
            jnp.zeros_like(device_total),
        )
        base_state = start_state + earlier_sum
        states_after = base_state[None] + running
        states_before = states_after - increment
        layer_in = states_before.astype(jnp.bfloat16)
    return states_after


def solution(mesh):
    return jax.shard_map(
        shards,
        mesh=mesh,
        in_specs=(
            P(("parts", "chan"), None),
            P(("parts", "tm", "sub"), "chan", None),
            P(),
            P(),
            P(),
            P(),
            P(),
            P("parts"),
            P("parts"),
        ),
        out_specs=P(("parts", "tm", "sub"), "chan", None),
        check_vma=False,
    )
```

profile of v0, /device:TPU:0, one launch (start us, length us, event | category | flops | bytes accessed | tf_op | source)
XLA Modules:
  0.0 128.8 jit_solution(10329179195908756646)
XLA Ops:
  1.1 4.9 %collective-permute-start = (bf16[4,3,2048]{2,1,0:T(4,128)(2,1)S(1)}, bf16[4,3,2048]{2,1,0:T(4,128)(2,1)S(1)}, u32[]{:S(2)}, u32[]{:S(2)}) collective-permute-start(bf16[4,3,2048]{2,1,0:T(4,128)(2,1)S(1)} %get-tuple-element.267), channel_id=1, source_target_pairs={{0,2},{1,3},{4,6},{5,7},{8,10},{9,11},{12,14},{13,15},{16,18},{17,... | collective-permute-start | bytes 147464 | tf_op jit(solution)/shard_map/ppermute | solution.py:14
  13.4 1.5 %pad_slice_fusion.30 = (bf16[4,8,32,64]{3,2,1,0:T(8,128)(2,1)S(1)}, bf16[4,8,32,64]{3,2,1,0:T(8,128)(2,1)}, bf16[4,8,32,64]{3,2,1,0:T(8,128)(2,1)}, bf16[4,8,32,...) fusion(bf16[4,10,32,64]{3,2,1,0:T(8,128)(2,1)S(1)} %reshape.67), kind=kLoop, calls=%fused_computation.43 | loop fusion | bytes 2293760 | tf_op jit(solution)/shard_map/slice | solution.py:47
  14.9 2.7 %concatenate.31 = bf16[4,8,32,576]{3,2,1,0:T(8,128)(2,1)S(1)} concatenate(bf16[4,8,32,64]{3,2,1,0:T(8,128)(2,1)} %get-tuple-element.263, bf16[4,8,32,64]{3,2,1,0:T(8,128)(2,1)} %get-tuple-element.262, bf16[4,8,32,64]{3,2,1,0:T(8,128)(2,1)} %get-tuple-element.257, bf16[4,8,32,64]{3,2,1,0:T(8,128)(2,1)} %get-tuple-element.258, bf16[4,8,32,64]{3,2,1,0:T(8,128)(2,1)} %get-tuple-element.261, ...), dimensions={3} | concatenate | bytes 2359296 | tf_op jit(solution)/shard_map/concatenate | solution.py:45
  17.7 2.1 %select_convert_fusion.1 = bf16[4,8,32,320]{3,2,1,0:T(8,128)(2,1)S(1)} fusion(bf16[4,8,32,576]{3,2,1,0:T(8,128)(2,1)S(1)} %concatenate.31, f32[4,320]{1,0:T(4,128)S(1)} %fusion.22, pred[8]{0:T(512)(128)(4,1)S(1)} %compare_and_fusion, bf16[576,320]{0,1:T(8,128)(2,1)} %param.15), kind=kOutput, calls=%fused_computation.7 | convolution fusion | flops 379781120 | bytes 2208776 | tf_op jit(solution)/shard_map/dot_general | solution.py:53
  19.8 2.4 %pad_slice_fusion.6 = (bf16[4,6,32,320]{3,2,1,0:T(8,128)(2,1)S(1)}, bf16[4,6,32,320]{3,2,1,0:T(8,128)(2,1)S(1)}, bf16[4,6,32,320]{3,2,1,0:T(8,128)(2,1)}, bf16[4...) fusion(bf16[4,8,32,320]{3,2,1,0:T(8,128)(2,1)S(1)} %select_conv, ...), kind=kLoop, calls=%fused_computation.17 | loop fusion | bytes 6979584 | tf_op jit(solution)/shard_map/slice | solution.py:47
  22.2 8.1 %concatenate.32 = bf16[4,6,32,2880]{3,2,1,0:T(8,128)(2,1)} concatenate(bf16[4,6,32,320]{3,2,1,0:T(8,128)(2,1)} %get-tuple-element.228, bf16[4,6,32,320]{3,2,1,0:T(8,128)(2,1)} %get-tuple-element.227, bf16[4,6,32,320]{3,2,1,0:T(8,128)(2,1)S(1)} %get-tuple-element.221, bf16[4,6,32,320]{3,2,1,0:T(8,128)(2,1)} %get-tuple-element.222, bf16[4,6,32,320]{3,2,1,0:T(8,128)(2,1)} %get-tuple-element.226, ...), dimensions={3} | concatenate | bytes 8847360 | tf_op jit(solution)/shard_map/concatenate | solution.py:45
  30.3 4.9 %select_convert_fusion.3 = bf16[4,6,32,320]{3,2,1,0:T(8,128)(2,1)S(1)} fusion(bf16[4,6,32,2880]{3,2,1,0:T(8,128)(2,1)} %concatenate.32, bf16[2880,320]{0,1:T(8,128)(2,1)S(1)} %copy-done, pred[6]{0:T(512)(128)(4,1)S(1)} %compare_and_fusion.1), kind=kOutput, calls=%fused_computation.9 | convolution fusion | flops 1417052160 | bytes 6758406 | tf_op jit(solution)/shard_map/dot_general | solution.py:53
  35.2 1.5 %pad_slice_fusion.18 = (bf16[4,4,32,320]{3,2,1,0:T(8,128)(2,1)S(1)}, bf16[4,4,32,320]{3,2,1,0:T(8,128)(2,1)S(1)}, bf16[4,4,32,320]{3,2,1,0:T(8,128)(2,1)S(1)}, b...) fusion(bf16[4,6,32,320]{3,2,1,0:T(8,128)(2,1)S(1)} %select_conv, ...), kind=kLoop, calls=%fused_computation.29 | loop fusion | bytes 4718592 | tf_op jit(solution)/shard_map/slice | solution.py:47
  36.8 5.8 %concatenate.33 = bf16[4,4,32,2880]{3,2,1,0:T(8,128)(2,1)} concatenate(bf16[4,4,32,320]{3,2,1,0:T(8,128)(2,1)} %get-tuple-element.246, bf16[4,4,32,320]{3,2,1,0:T(8,128)(2,1)} %get-tuple-element.245, bf16[4,4,32,320]{3,2,1,0:T(8,128)(2,1)S(1)} %get-tuple-element.239, bf16[4,4,32,320]{3,2,1,0:T(8,128)(2,1)S(1)} %get-tuple-element.240, bf16[4,4,32,320]{3,2,1,0:T(8,128)(2,1)} %get-tuple-element.244, ...), dimensions={3} | concatenate | bytes 5898240 | tf_op jit(solution)/shard_map/concatenate | solution.py:45
  42.6 2.9 %fusion.29 = f32[512,64]{0,1:T(8,128)S(1)} fusion(bf16[512,2880]{1,0:T(8,128)(2,1)} %bitcast.49, bf16[2880,64]{0,1:T(8,128)(2,1)} %param.17), kind=kOutput, calls=%fused_computation.78 | convolution fusion | flops 188743680 | bytes 3448832 | tf_op jit(solution)/shard_map/dot_general | solution.py:53
  48.0 17.5 %all_gather.6 = f32[8,4,2048]{2,1,0:T(4,128)S(1)} all-gather(f32[1,4,2048]{2,1,0:T(4,128)S(1)} %slice.308), channel_id=1, replica_groups=mesh['parts'=2,'tm'=4,'chan'=2,'sub'=2] {'tm','sub'}, dimensions={0}, use_global_device_ids=true | all-gather | bytes 294912 | tf_op jit(solution)/shard_map/all_gather | solution.py:30
  66.0 3.5 %collective-permute-start.3 = (bf16[4,3,2048]{2,1,0:T(4,128)(2,1)S(1)}, bf16[4,3,2048]{2,1,0:T(4,128)(2,1)S(1)}, u32[]{:S(2)}, u32[]{:S(2)}) collective-permute-start(bf16[4,3,2048]{2,1,0:T(4,128)(2,1)S(1)} %get-tuple-element.265), channel_id=1, source_target_pairs={{0,2},{1,3},{4,6},{5,7},{8,10},{9,11},{12,14},{13,15},{16,18},{17,... | collective-permute-start | bytes 147464 | tf_op jit(solution)/shard_map/ppermute | solution.py:14
  69.5 1.5 %collective-permute-start.4 = (bf16[4,3,2048]{2,1,0:T(4,128)(2,1)S(1)}, bf16[4,3,2048]{2,1,0:T(4,128)(2,1)S(1)}, u32[]{:S(2)}, u32[]{:S(2)}) collective-permute-start(bf16[4,3,2048]{2,1,0:T(4,128)(2,1)S(1)} %get-tuple-element.266), channel_id=1, source_target_pairs={{2,0},{3,1},{6,4},{7,5},{10,8},{11,9},{14,12},{15,13},{18,16},{19,... | collective-permute-start | bytes 147464 | tf_op jit(solution)/shard_map/ppermute | solution.py:17
  71.4 4.3 %collective-permute-done.4 = bf16[4,3,2048]{2,1,0:T(4,128)(2,1)S(1)} collective-permute-done((bf16[4,3,2048]{2,1,0:T(4,128)(2,1)S(1)}, bf16[4,3,2048]{2,1,0:T(4,128)(2,1)S(1)}, u32[]{:S(2)}, u32[]{:S(2)}) %collective-permute-start.4) | collective-permute-done | bytes 49184 | tf_op jit(solution)/shard_map/ppermute | solution.py:17
  76.2 1.5 %pad_slice_fusion.24 = (bf16[4,8,32,64]{3,2,1,0:T(8,128)(2,1)S(1)}, bf16[4,8,32,64]{3,2,1,0:T(8,128)(2,1)}, bf16[4,8,32,64]{3,2,1,0:T(8,128)(2,1)}, bf16[4,8,32,...) fusion(bf16[4,10,32,64]{3,2,1,0:T(8,128)(2,1)S(1)} %reshape.68), kind=kLoop, calls=%fused_computation.37 | loop fusion | bytes 2293760 | tf_op jit(solution)/shard_map/slice | solution.py:47
  77.6 2.7 %concatenate.36 = bf16[4,8,32,576]{3,2,1,0:T(8,128)(2,1)S(1)} concatenate(bf16[4,8,32,64]{3,2,1,0:T(8,128)(2,1)} %get-tuple-element.254, bf16[4,8,32,64]{3,2,1,0:T(8,128)(2,1)} %get-tuple-element.253, bf16[4,8,32,64]{3,2,1,0:T(8,128)(2,1)} %get-tuple-element.248, bf16[4,8,32,64]{3,2,1,0:T(8,128)(2,1)} %get-tuple-element.249, bf16[4,8,32,64]{3,2,1,0:T(8,128)(2,1)} %get-tuple-element.252, ...), dimensions={3} | concatenate | bytes 2359296 | tf_op jit(solution)/shard_map/concatenate | solution.py:45
  80.4 2.1 %select_convert_fusion = bf16[4,8,32,320]{3,2,1,0:T(8,128)(2,1)S(1)} fusion(bf16[4,8,32,576]{3,2,1,0:T(8,128)(2,1)S(1)} %concatenate.36, f32[4,320]{1,0:T(4,128)S(1)} %fusion.22, pred[8]{0:T(512)(128)(4,1)S(1)} %compare_and_fusion, bf16[576,320]{0,1:T(8,128)(2,1)} %param.15), kind=kOutput, calls=%fused_computation.6 | convolution fusion | flops 379781120 | bytes 2208776 | tf_op jit(solution)/shard_map/dot_general | solution.py:53
  82.5 2.4 %pad_slice_fusion = (bf16[4,6,32,320]{3,2,1,0:T(8,128)(2,1)S(1)}, bf16[4,6,32,320]{3,2,1,0:T(8,128)(2,1)S(1)}, bf16[4,6,32,320]{3,2,1,0:T(8,128)(2,1)}, bf16[4,6...) fusion(bf16[4,8,32,320]{3,2,1,0:T(8,128)(2,1)S(1)} %select_conv, ...), kind=kLoop, calls=%fused_computation.11 | loop fusion | bytes 6979584 | tf_op jit(solution)/shard_map/slice | solution.py:47
  84.9 8.1 %concatenate.37 = bf16[4,6,32,2880]{3,2,1,0:T(8,128)(2,1)} concatenate(bf16[4,6,32,320]{3,2,1,0:T(8,128)(2,1)} %get-tuple-element.219, bf16[4,6,32,320]{3,2,1,0:T(8,128)(2,1)} %get-tuple-element.218, bf16[4,6,32,320]{3,2,1,0:T(8,128)(2,1)S(1)} %get-tuple-element.212, bf16[4,6,32,320]{3,2,1,0:T(8,128)(2,1)} %get-tuple-element.213, bf16[4,6,32,320]{3,2,1,0:T(8,128)(2,1)} %get-tuple-element.217, ...), dimensions={3} | concatenate | bytes 8847360 | tf_op jit(solution)/shard_map/concatenate | solution.py:45
  93.0 4.9 %select_convert_fusion.2 = bf16[4,6,32,320]{3,2,1,0:T(8,128)(2,1)S(1)} fusion(bf16[4,6,32,2880]{3,2,1,0:T(8,128)(2,1)} %concatenate.37, bf16[2880,320]{0,1:T(8,128)(2,1)S(1)} %copy-done, pred[6]{0:T(512)(128)(4,1)S(1)} %compare_and_fusion.1), kind=kOutput, calls=%fused_computation.8 | convolution fusion | flops 1417052160 | bytes 6758406 | tf_op jit(solution)/shard_map/dot_general | solution.py:53
  98.0 1.5 %pad_slice_fusion.12 = (bf16[4,4,32,320]{3,2,1,0:T(8,128)(2,1)S(1)}, bf16[4,4,32,320]{3,2,1,0:T(8,128)(2,1)S(1)}, bf16[4,4,32,320]{3,2,1,0:T(8,128)(2,1)S(1)}, b...) fusion(bf16[4,6,32,320]{3,2,1,0:T(8,128)(2,1)S(1)} %select_conv, ...), kind=kLoop, calls=%fused_computation.23 | loop fusion | bytes 4718592 | tf_op jit(solution)/shard_map/slice | solution.py:47
  99.5 5.8 %concatenate.38 = bf16[4,4,32,2880]{3,2,1,0:T(8,128)(2,1)} concatenate(bf16[4,4,32,320]{3,2,1,0:T(8,128)(2,1)} %get-tuple-element.237, bf16[4,4,32,320]{3,2,1,0:T(8,128)(2,1)} %get-tuple-element.236, bf16[4,4,32,320]{3,2,1,0:T(8,128)(2,1)S(1)} %get-tuple-element.230, bf16[4,4,32,320]{3,2,1,0:T(8,128)(2,1)S(1)} %get-tuple-element.231, bf16[4,4,32,320]{3,2,1,0:T(8,128)(2,1)} %get-tuple-element.235, ...), dimensions={3} | concatenate | bytes 5898240 | tf_op jit(solution)/shard_map/concatenate | solution.py:45
  105.3 2.9 %fusion.30 = f32[512,64]{0,1:T(8,128)S(1)} fusion(bf16[512,2880]{1,0:T(8,128)(2,1)} %bitcast.50, bf16[2880,64]{0,1:T(8,128)(2,1)} %param.17), kind=kOutput, calls=%fused_computation.79 | convolution fusion | flops 188743680 | bytes 3448832 | tf_op jit(solution)/shard_map/dot_general | solution.py:53
  110.7 17.0 %all_gather.7 = f32[8,4,2048]{2,1,0:T(4,128)S(1)} all-gather(f32[1,4,2048]{2,1,0:T(4,128)S(1)} %slice.322), channel_id=1, replica_groups=mesh['parts'=2,'tm'=4,'chan'=2,'sub'=2] {'tm','sub'}, dimensions={0}, use_global_device_ids=true | all-gather | bytes 294912 | tf_op jit(solution)/shard_map/all_gather | solution.py:30
  (71 shorter events, 15.4 us)
Async XLA Ops:
  0.0 30.3 %copy-start = (bf16[2880,320]{0,1:T(8,128)(2,1)S(1)}, bf16[2880,320]{0,1:T(8,128)(2,1)}, u32[]{:S(2)}) copy-start(bf16[2880,320]{0,1:T(8,128)(2,1)} %param.16) | copy-start | bytes 5529604
  1.1 10.0 %collective-permute-start = (bf16[4,3,2048]{2,1,0:T(4,128)(2,1)S(1)}, bf16[4,3,2048]{2,1,0:T(4,128)(2,1)S(1)}, u32[]{:S(2)}, u32[]{:S(2)}) collective-permute-start(bf16[4,3,2048]{2,1,0:T(4,128)(2,1)S(1)} %get-tuple-element.267), channel_id=1, source_target_pairs={{0,2},{1,3},{4,6},{5,7},{8,10},{9,11},{12,14},{13,15},{16,18},{17,... | collective-permute-start | bytes 147464 | tf_op jit(solution)/shard_map/ppermute | solution.py:14
  6.0 6.2 %collective-permute-start.1 = (bf16[4,3,2048]{2,1,0:T(4,128)(2,1)S(1)}, bf16[4,3,2048]{2,1,0:T(4,128)(2,1)S(1)}, u32[]{:S(2)}, u32[]{:S(2)}) collective-permute-start(bf16[4,3,2048]{2,1,0:T(4,128)(2,1)S(1)} %get-tuple-element.268), channel_id=1, source_target_pairs={{2,0},{3,1},{6,4},{7,5},{10,8},{11,9},{14,12},{15,13},{18,16},{19,... | collective-permute-start | bytes 147464 | tf_op jit(solution)/shard_map/ppermute | solution.py:17
  45.7 2.1 %collective-permute-start.2 = (f32[4,2048]{1,0:T(4,128)S(1)}, f32[4,2048]{1,0:T(4,128)S(1)}, u32[]{:S(2)}, u32[]{:S(2)}) collective-permute-start(f32[4,2048]{1,0:T(4,128)S(1)} %squeeze.24), channel_id=1, source_target_pairs={{0,1},{1,4},{4,5},{5,8},{8,9},{9,12},{12,13},{2,3},{3,6},{6,7},{7,... | collective-permute-start | bytes 98312 | tf_op jit(solution)/shard_map/ppermute | solution.py:25
  47.1 18.8 %copy-start.1 = (f32[4,2048]{1,0:T(4,128)S(1)}, f32[4,2048]{1,0:T(4,128)}, u32[]{:S(2)}) copy-start(f32[4,2048]{1,0:T(4,128)} %param.13) | copy-start | bytes 98308
  66.0 5.4 %collective-permute-start.3 = (bf16[4,3,2048]{2,1,0:T(4,128)(2,1)S(1)}, bf16[4,3,2048]{2,1,0:T(4,128)(2,1)S(1)}, u32[]{:S(2)}, u32[]{:S(2)}) collective-permute-start(bf16[4,3,2048]{2,1,0:T(4,128)(2,1)S(1)} %get-tuple-element.265), channel_id=1, source_target_pairs={{0,2},{1,3},{4,6},{5,7},{8,10},{9,11},{12,14},{13,15},{16,18},{17,... | collective-permute-start | bytes 147464 | tf_op jit(solution)/shard_map/ppermute | solution.py:14
  69.5 6.2 %collective-permute-start.4 = (bf16[4,3,2048]{2,1,0:T(4,128)(2,1)S(1)}, bf16[4,3,2048]{2,1,0:T(4,128)(2,1)S(1)}, u32[]{:S(2)}, u32[]{:S(2)}) collective-permute-start(bf16[4,3,2048]{2,1,0:T(4,128)(2,1)S(1)} %get-tuple-element.266), channel_id=1, source_target_pairs={{2,0},{3,1},{6,4},{7,5},{10,8},{11,9},{14,12},{15,13},{18,16},{19,... | collective-permute-start | bytes 147464 | tf_op jit(solution)/shard_map/ppermute | solution.py:17
  108.4 2.1 %collective-permute-start.5 = (f32[4,2048]{1,0:T(4,128)S(1)}, f32[4,2048]{1,0:T(4,128)S(1)}, u32[]{:S(2)}, u32[]{:S(2)}) collective-permute-start(f32[4,2048]{1,0:T(4,128)S(1)} %squeeze.25), channel_id=1, source_target_pairs={{0,1},{1,4},{4,5},{5,8},{8,9},{9,12},{12,13},{2,3},{3,6},{6,7},{7,... | collective-permute-start | bytes 98312 | tf_op jit(solution)/shard_map/ppermute | solution.py:25
where the time goes:
time: 131 us; the launch traced here: 129 us
  local copies, waits for them, and re-layouts  48 us (37%)
  blocking collectives  34.6 us (26%)
  matrix products  22.2 us (17%)
  starting transfers between devices  13.7 us (10%)
  waiting for transfers between devices  6.27 us (5%)
  other arithmetic  2.67 us (2%)
    all_gather x2, blocking collectives, carried_in(): everything = lax.all_gather(array, axis)  34.6 us
    concatenate x6, local copies, waits for them, and re-layouts, conv_valid(): jnp.concatenate([padded[:, row_off:row_off + rows_out, col_off:col_off +...  33.2 us
    dot_general x6, matrix products, conv_valid(): jnp.dot(patches.reshape(-1, 9 * channels), weight, preferred_element_type...  19.9 us
    slice x6, local copies, waits for them, and re-layouts, conv_valid(): padded[:, row_off:row_off + rows_out, col_off:col_off + width_in, :]  10.9 us
    ppermute x2, starting transfers between devices, padded_2(): lax.ppermute(lax.slice_in_dim(block, block.shape[dim] - width, None, axis...  8.38 us
    ppermute x2, waiting for transfers between devices, padded_2(): lax.ppermute(lax.slice_in_dim(block, 0, width, axis=dim), axis, backward)  5.33 us
    ppermute x2, starting transfers between devices, padded_2(): lax.ppermute(lax.slice_in_dim(block, 0, width, axis=dim), axis, backward)  2.76 us
  transfers between devices with their start and end apart: 6, of which 5 were waited for; matrix products, arithmetic and copies ran while one was open for 3% of the time, Pallas kernels for 0%

commit v1 on v0

v1 whole, which is shorter than its diff:
```python
import jax
import jax.numpy as jnp
from jax import lax
from jax.experimental import pallas as pl
from jax.experimental.pallas import tpu as pltpu
from jax.sharding import PartitionSpec as P

ITERS = 2
TIME_AXES = ("tm", "sub")


def padded_2(block, sides, width):
    for axis, dim in sides:
        count = lax.axis_size(axis)
        forward = [(i, i + 1) for i in range(count - 1)]
        backward = [(target, source) for source, target in forward]
        low = lax.ppermute(
            lax.slice_in_dim(block, block.shape[dim] - width, None, axis=dim), axis, forward
        )
        high = lax.ppermute(lax.slice_in_dim(block, 0, width, axis=dim), axis, backward)
        block = jnp.concatenate([low, block, high], axis=dim)
    return block


def conv3x3(src_ref, w_ref, rows_out):
    steps, _, columns, channels_in = src_ref.shape
    channels_out = w_ref.shape[-1]
    size = steps * rows_out * columns
    taps = []
    for col_off in range(3):
        acc = None
        for row_off in range(3):
            patch = src_ref[:, row_off : row_off + rows_out].reshape(size, channels_in)
            part = jnp.dot(patch, w_ref[row_off * 3 + col_off], preferred_element_type=jnp.float32)
            acc = part if acc is None else acc + part
        taps.append(acc)
    column = lax.broadcasted_iota(jnp.int32, (steps * rows_out, columns, channels_out), 1)
    column = column.reshape(size, channels_out)
    left = jnp.where(column == 0, 0.0, pltpu.roll(taps[0], 1, 0))
    right = jnp.where(column == columns - 1, 0.0, pltpu.roll(taps[2], size - 1, 0))
    return (left + taps[1] + right).reshape(steps, rows_out, columns, channels_out)


def silu(v):
    return v / (1.0 + jnp.exp(-v))


def row_valid(shape, first_row, total_rows):
    rows = first_row + lax.broadcasted_iota(jnp.int32, shape, 1)
    return (rows >= 0) & (rows < total_rows)


def drift_kernel(total_rows, first_ref, x_ref, emb_ref, w1_ref, w2_ref, w3_ref, out_ref, h1_ref, h2_ref):
    first_row = first_ref[0]
    steps, rows_1, columns, hidden = h1_ref.shape
    rows_2 = h2_ref.shape[1]
    act = conv3x3(x_ref, w1_ref, rows_1) + emb_ref[...][:, None, None, :]
    act = jnp.where(row_valid(act.shape, first_row, total_rows), silu(act), 0.0)
    h1_ref[...] = act.astype(jnp.bfloat16)
    act = conv3x3(h1_ref, w2_ref, rows_2)
    act = jnp.where(row_valid(act.shape, first_row + 1, total_rows), silu(act), 0.0)
    h2_ref[...] = act.astype(jnp.bfloat16)
    out_ref[...] = conv3x3(h2_ref, w3_ref, out_ref.shape[1])


def drift(layer_in, embed, w_in, w_mid, w_out):
    steps_dev, tile_rows, merged = layer_in.shape
    channels = w_out.shape[1]
    hidden = w_in.shape[1]
    columns = merged // channels
    rimmed = padded_2(layer_in, (("chan", 1),), 3)
    first_row = lax.axis_index("chan") * tile_rows - 2
    total_rows = tile_rows * lax.axis_size("chan")
    x = rimmed.reshape(steps_dev, tile_rows + 6, columns, channels)
    w1 = w_in.reshape(9, channels, hidden)
    w2 = w_mid.reshape(9, hidden, hidden)
    w3 = w_out.reshape(9, hidden, channels)
    rows = (tile_rows + 4) + (tile_rows + 2) + tile_rows
    flops = 2 * steps_dev * columns * 9 * hidden * (channels * (tile_rows + 4) + hidden * (tile_rows + 2) + channels * tile_rows)
    vmem = pl.BlockSpec(memory_space=pltpu.VMEM)
    out = pl.pallas_call(
        lambda *refs: drift_kernel(total_rows, *refs),
        out_shape=jax.ShapeDtypeStruct((steps_dev, tile_rows, columns, channels), jnp.float32),
        in_specs=[pl.BlockSpec(memory_space=pltpu.SMEM)] + [vmem] * 5,
        out_specs=vmem,
        scratch_shapes=[
            pltpu.VMEM((steps_dev, tile_rows + 4, columns, hidden), jnp.bfloat16),
            pltpu.VMEM((steps_dev, tile_rows + 2, columns, hidden), jnp.bfloat16),
        ],
        compiler_params=pltpu.CompilerParams(vmem_limit_bytes=48 * 1024 * 1024),
        cost_estimate=pl.CostEstimate(
            flops=flops,
            transcendentals=steps_dev * columns * hidden * rows,
            bytes_accessed=2 * (w1.size + w2.size + w3.size) + 2 * x.size + 4 * steps_dev * tile_rows * merged,
        ),
    )(first_row.reshape(1).astype(jnp.int32), x, embed, w1, w2, w3)
    return out.reshape(steps_dev, tile_rows, merged)


def shifted(array, by):
    devices = lax.axis_size(TIME_AXES)
    pairs = [(i, i + by) for i in range(devices - by)]
    return lax.ppermute(array, TIME_AXES, pairs)


def scan_earlier(total, carried):
    devices = lax.axis_size(TIME_AXES)
    if carried is None:
        got = shifted(total, 1)
        moved = None
    else:
        both = shifted(jnp.stack([total, carried]), 1)
        got, moved = both[0], both[1]
    earlier = got
    running = total + got
    by = 2
    while by < devices:
        got = shifted(running, by)
        earlier = earlier + got
        if by * 2 < devices:
            running = running + got
        by *= 2
    return earlier, moved


def shards(start_state, guess, w_in, w_mid, w_out, time_embed, levels, plan, offset):
    steps_dev = guess.shape[0]
    devices = lax.axis_size(TIME_AXES)
    time_index = lax.axis_index(TIME_AXES)
    first_step = time_index * steps_dev
    window_ids = lax.dynamic_slice_in_dim(plan, offset[0] + first_step, steps_dev + 1)
    after_id = lax.dynamic_slice_in_dim(
        plan, jnp.minimum(offset[0] + first_step + steps_dev + 1, plan.shape[0] - 1), 1
    )
    all_ids = jnp.concatenate([window_ids, after_id])
    one_hot = all_ids[:, None] == jnp.arange(levels.shape[0], dtype=jnp.int32)[None, :]
    noise = jnp.dot(one_hot.astype(jnp.float32), levels, precision=lax.Precision.HIGHEST)
    step_size = noise[1 : steps_dev + 1] - noise[:steps_dev]
    next_step = jnp.where(time_index < devices - 1, noise[steps_dev + 1] - noise[steps_dev], 0.0)
    embed = jnp.dot(
        one_hot[:steps_dev].astype(jnp.bfloat16), time_embed, preferred_element_type=jnp.float32
    )
    factor = jnp.where(first_step + jnp.arange(steps_dev, dtype=jnp.int32) == 0, 1.0, 1.5).astype(
        jnp.float32
    )
    layer_in = guess
    states_after = None
    for sweep in range(ITERS):
        last_sweep = sweep == ITERS - 1
        drift_now = drift(layer_in, embed, w_in, w_mid, w_out)
        earlier_local = jnp.concatenate([jnp.zeros_like(drift_now[:1]), drift_now[:-1]], axis=0)
        increment = step_size[:, None, None] * (factor[:, None, None] * drift_now - 0.5 * earlier_local)
        running = jnp.cumsum(increment, axis=0)
        handed_on = running[-1] - 0.5 * next_step * drift_now[-1]
        earlier_sum, previous = scan_earlier(handed_on, None if last_sweep else drift_now[-1])
        states_after = (start_state + earlier_sum)[None] + running
        if not last_sweep:
            first_extra = -0.5 * step_size[0] * previous
            states_before = states_after - increment
            states_before = states_before.at[0].add(-first_extra)
            layer_in = states_before.astype(jnp.bfloat16)
    return states_after


def solution(mesh):
    return jax.shard_map(
        shards,
        mesh=mesh,
        in_specs=(
            P(("parts", "chan"), None),
            P(("parts", "tm", "sub"), "chan", None),
            P(),
            P(),
            P(),
            P(),
            P(),
            P("parts"),
            P("parts"),
        ),
        out_specs=P(("parts", "tm", "sub"), "chan", None),
        check_vma=False,
    )
```

time: 131 us -> 91.5 us (0.70); the launches traced: 129 us -> 90.7 us
  blocking collectives: 34.6 us -> 0 us
  local copies, waits for them, and re-layouts: 48 us -> 18.5 us
  starting transfers between devices: 13.7 us -> 39.3 us
  matrix products: 22.2 us -> 1.18 us
  Pallas kernels: 0 us -> 13.7 us
  waiting for transfers between devices: 6.27 us -> 12.6 us
    all_gather x2 -> x0, blocking collectives: 34.6 us -> none  [carried_in(): everything = lax.all_gather(array, axis)]
    concatenate x6 -> x0, local copies, waits for them, and re-layouts: 33.2 us -> none  [conv_valid(): jnp.concatenate([padded[:, row_off:row_off + rows_out, col_off:col_off +...]
    ppermute x2 -> x6, starting transfers between devices: 2.58 us -> 27.2 us  [shifted(): return lax.ppermute(array, TIME_AXES, pairs)]
    dot_general x7 -> x1, matrix products: 21.3 us -> 0.32 us  [shards(): jnp.dot(one_hot[:steps_dev].astype(jnp.bfloat16), time_embed, preferred_e...]
    pallas_call x0 -> x2, Pallas kernels: none -> 13.7 us  [drift(): pl.pallas_call(lambda *refs: drift_kernel(total_rows, *refs), out_shape=j...]
    unnamed x5 -> x18, local copies, waits for them, and re-layouts: 0.02 us -> 11.7 us
    slice x18 -> x5, local copies, waits for them, and re-layouts: 11.6 us -> 2.56 us  [the longest x4 1.88 us: shards(): drift_now[:-1]]
    ppermute x2 -> x6, waiting for transfers between devices: 0.5 us -> 7.91 us  [shifted(): return lax.ppermute(array, TIME_AXES, pairs)]
  transfers between devices with their start and end apart: 6 -> 10, of which waited for: 5 -> 8; matrix products, arithmetic and copies ran while one was open for 3% -> 14% of each run, Pallas kernels for 0% -> 0%
where the time goes in v1:
time: 91.5 us; the launch traced here: 90.7 us
  starting transfers between devices  39.3 us (43%)
  local copies, waits for them, and re-layouts  18.5 us (20%)
  Pallas kernels  13.7 us (15%)
  waiting for transfers between devices  12.6 us (14%)
  other arithmetic  3.15 us (3%)
  between operations  2.25 us (2%)
  matrix products  1.18 us (1%)
    ppermute x6, starting transfers between devices, shifted(): return lax.ppermute(array, TIME_AXES, pairs)  27.2 us
    pallas_call x2, Pallas kernels, drift(): pl.pallas_call(lambda *refs: drift_kernel(total_rows, *refs), out_shape=j...  13.7 us
    unnamed x18, local copies, waits for them, and re-layouts  11.7 us
    ppermute x2, starting transfers between devices, padded_2(): lax.ppermute(lax.slice_in_dim(block, block.shape[dim] - width, None, axis...  9.42 us
    ppermute x6, waiting for transfers between devices, shifted(): return lax.ppermute(array, TIME_AXES, pairs)  7.91 us
    ppermute x2, waiting for transfers between devices, padded_2(): lax.ppermute(lax.slice_in_dim(block, 0, width, axis=dim), axis, backward)  4.28 us
    ppermute x2, starting transfers between devices, padded_2(): lax.ppermute(lax.slice_in_dim(block, 0, width, axis=dim), axis, backward)  2.76 us
    slice x4, local copies, waits for them, and re-layouts, shards(): drift_now[:-1]  1.88 us
  transfers between devices with their start and end apart: 10, of which 8 were waited for; matrix products, arithmetic and copies ran while one was open for 14% of the time, Pallas kernels for 0%

profile of v1, /device:TPU:0, one launch (start us, length us, event | category | flops | bytes accessed | tf_op | source)
XLA Modules:
  0.0 90.7 jit_solution(7987075004511623750)
XLA Ops:
  1.0 4.9 %collective-permute-start = (bf16[4,3,2048]{2,1,0:T(4,128)(2,1)S(1)}, bf16[4,3,2048]{2,1,0:T(4,128)(2,1)S(1)}, u32[]{:S(2)}, u32[]{:S(2)}) collective-permute-start(bf16[4,3,2048]{2,1,0:T(4,128)(2,1)S(1)} %get-tuple-element.21), channel_id=1, source_target_pairs={{0,2},{1,3},{4,6},{5,7},{8,10},{9,11},{12,14},{13,15},{16,18},{17,... | collective-permute-start | bytes 147464 | tf_op jit(solution)/shard_map/ppermute | solution.py:17
  5.9 1.3 %collective-permute-start.1 = (bf16[4,3,2048]{2,1,0:T(4,128)(2,1)S(1)}, bf16[4,3,2048]{2,1,0:T(4,128)(2,1)S(1)}, u32[]{:S(2)}, u32[]{:S(2)}) collective-permute-start(bf16[4,3,2048]{2,1,0:T(4,128)(2,1)S(1)} %get-tuple-element.22), channel_id=1, source_target_pairs={{2,0},{3,1},{6,4},{7,5},{10,8},{11,9},{14,12},{15,13},{18,16},{19,... | collective-permute-start | bytes 147464 | tf_op jit(solution)/shard_map/ppermute | solution.py:20
  7.9 1.2 %dynamic_slice.7 = s32[1]{0:T(128)} dynamic-slice(s32[65]{0:T(128)} %param.18, s32[]{:T(128)S(6)} %select_n.19), dynamic_slice_sizes={1} | dynamic-slice | bytes 12 | tf_op jit(solution)/shard_map/dynamic_slice | solution.py:132
  12.6 2.0 %copy.14 = bf16[576,320]{1,0:T(8,128)(2,1)} copy(bf16[576,320]{0,1:T(8,128)(2,1)} %param.13) | data formatting | bytes 737280 | tf_op args[2]
  14.5 2.2 %copy.16 = bf16[2880,64]{1,0:T(8,128)(2,1)} copy(bf16[2880,64]{0,1:T(8,128)(2,1)} %param.15) | data formatting | bytes 737280 | tf_op args[4]
  16.7 3.3 %copy.15 = bf16[2880,320]{1,0:T(8,128)(2,1)S(1)} copy(bf16[2880,320]{0,1:T(8,128)(2,1)} %param.14) | data formatting | bytes 3686400 | tf_op args[3]
  21.8 1.1 %copy-done.1 = bf16[2880,64]{1,0:T(8,128)(2,1)S(1)} copy-done((bf16[2880,64]{1,0:T(8,128)(2,1)S(1)}, bf16[2880,64]{1,0:T(8,128)(2,1)}, u32[]{:S(2)}) %copy-start.1) | copy-done | bytes 368664
  23.9 6.9 %shard_map.91 = f32[4,4,32,64]{3,2,1,0:T(8,128)S(1)} custom-call(s32[1]{0:T(128)} %bitcast.3.refs_0_, bf16[4,10,32,64]{3,2,1,0:T(8,128)(2,1)S(1)} %reshape.102.refs_1_, f32[4,320]{1,0:T(4,128)S(1)} %fusion.14.refs_2_, bf16[9,64,320]{2,1,0:T(8,128)(2,1)S(1)} %bitcast.49, bf16[9,320,320]{2,1,0:T(8,128)(2,1)S(1)} %bitcast.45, bf16[9,320,64]{2,1,0:T(8,128)(2,1)S(1)} %bitcast.47), custom_call_target="tpu_custom_call" | custom-call | flops 1981808640 | bytes 2875392 | tf_op jit(solution)/shard_map/pallas_call | solution.py:81
  31.7 1.0 %slice.91 = f32[3,4,2048]{2,1,0:T(4,128)S(1)} reshape(f32[3,4,32,64]{3,2,1,0:T(8,128)} %slice.107) | data formatting | bytes 196608 | tf_op jit(solution)/shard_map/slice | solution.py:151
  33.0 1.5 %collective-permute-start.2 = (f32[2,4,2048]{2,1,0:T(4,128)S(1)}, f32[2,4,2048]{2,1,0:T(4,128)S(1)}, u32[]{:S(2)}, u32[]{:S(2)}) collective-permute-start(f32[2,4,2048]{2,1,0:T(4,128)S(1)} %pad_maximum_fusion.2), channel_id=1, source_target_pairs={{0,1},{1,4},{4,5},{5,8},{8,9},{9,12},{12,13},{2,3},{3,6},{6,7},{7,... | collective-permute-start | bytes 196616 | tf_op jit(solution)/shard_map/ppermute | solution.py:103
  35.3 6.7 %collective-permute-start.3 = (f32[4,2048]{1,0:T(4,128)S(1)}, f32[4,2048]{1,0:T(4,128)S(1)}, u32[]{:S(2)}, u32[]{:S(2)}) collective-permute-start(f32[4,2048]{1,0:T(4,128)S(1)} %fusion.13), channel_id=1, source_target_pairs={{0,4},{1,5},{4,8},{5,9},{8,12},{9,13},{2,6},{3,7},{6,10},{7,11},{1... | collective-permute-start | bytes 98312 | tf_op jit(solution)/shard_map/ppermute | solution.py:103
  42.1 1.6 %collective-permute-done.3 = f32[4,2048]{1,0:T(4,128)S(1)} collective-permute-done((f32[4,2048]{1,0:T(4,128)S(1)}, f32[4,2048]{1,0:T(4,128)S(1)}, u32[]{:S(2)}, u32[]{:S(2)}) %collective-permute-start.3) | collective-permute-done | bytes 32800 | tf_op jit(solution)/shard_map/ppermute | solution.py:103
  43.6 5.2 %collective-permute-start.4 = (f32[4,2048]{1,0:T(4,128)S(1)}, f32[4,2048]{1,0:T(4,128)S(1)}, u32[]{:S(2)}, u32[]{:S(2)}) collective-permute-start(f32[4,2048]{1,0:T(4,128)S(1)} %add.96), channel_id=1, source_target_pairs={{0,8},{1,9},{4,12},{5,13},{2,10},{3,11},{6,14},{7,15},{16,24},{17,... | collective-permute-start | bytes 98312 | tf_op jit(solution)/shard_map/ppermute | solution.py:103
  48.9 1.5 %collective-permute-done.4 = f32[4,2048]{1,0:T(4,128)S(1)} collective-permute-done((f32[4,2048]{1,0:T(4,128)S(1)}, f32[4,2048]{1,0:T(4,128)S(1)}, u32[]{:S(2)}, u32[]{:S(2)}) %collective-permute-start.4) | collective-permute-done | bytes 32800 | tf_op jit(solution)/shard_map/ppermute | solution.py:103
  51.5 4.5 %collective-permute-start.5 = (bf16[4,3,2048]{2,1,0:T(4,128)(2,1)S(1)}, bf16[4,3,2048]{2,1,0:T(4,128)(2,1)S(1)}, u32[]{:S(2)}, u32[]{:S(2)}) collective-permute-start(bf16[4,3,2048]{2,1,0:T(4,128)(2,1)S(1)} %get-tuple-element.19), channel_id=1, source_target_pairs={{0,2},{1,3},{4,6},{5,7},{8,10},{9,11},{12,14},{13,15},{16,18},{17,... | collective-permute-start | bytes 147464 | tf_op jit(solution)/shard_map/ppermute | solution.py:17
  56.0 1.5 %collective-permute-start.6 = (bf16[4,3,2048]{2,1,0:T(4,128)(2,1)S(1)}, bf16[4,3,2048]{2,1,0:T(4,128)(2,1)S(1)}, u32[]{:S(2)}, u32[]{:S(2)}) collective-permute-start(bf16[4,3,2048]{2,1,0:T(4,128)(2,1)S(1)} %get-tuple-element.20), channel_id=1, source_target_pairs={{2,0},{3,1},{6,4},{7,5},{10,8},{11,9},{14,12},{15,13},{18,16},{19,... | collective-permute-start | bytes 147464 | tf_op jit(solution)/shard_map/ppermute | solution.py:20
  57.9 4.3 %collective-permute-done.6 = bf16[4,3,2048]{2,1,0:T(4,128)(2,1)S(1)} collective-permute-done((bf16[4,3,2048]{2,1,0:T(4,128)(2,1)S(1)}, bf16[4,3,2048]{2,1,0:T(4,128)(2,1)S(1)}, u32[]{:S(2)}, u32[]{:S(2)}) %collective-permute-start.6) | collective-permute-done | bytes 49184 | tf_op jit(solution)/shard_map/ppermute | solution.py:20
  62.7 1.1 %copy-done.2 = bf16[2880,64]{1,0:T(8,128)(2,1)S(1)} copy-done((bf16[2880,64]{1,0:T(8,128)(2,1)S(1)}, bf16[2880,64]{1,0:T(8,128)(2,1)}, u32[]{:S(2)}) %copy-start.2) | copy-done | bytes 368664
  64.8 6.9 %shard_map.92 = f32[4,4,32,64]{3,2,1,0:T(8,128)S(1)} custom-call(s32[1]{0:T(128)} %bitcast.3.refs_0_, bf16[4,10,32,64]{3,2,1,0:T(8,128)(2,1)S(1)} %reshape.103.refs_1_, f32[4,320]{1,0:T(4,128)S(1)} %fusion.14.refs_2_, bf16[9,64,320]{2,1,0:T(8,128)(2,1)S(1)} %bitcast.50, bf16[9,320,320]{2,1,0:T(8,128)(2,1)S(1)} %bitcast.46, bf16[9,320,64]{2,1,0:T(8,128)(2,1)S(1)} %bitcast.48), custom_call_target="tpu_custom_call" | custom-call | flops 1981808640 | bytes 2875392 | tf_op jit(solution)/shard_map/pallas_call | solution.py:81
  72.2 1.3 %collective-permute-start.7 = (f32[4,2048]{1,0:T(4,128)S(1)}, f32[4,2048]{1,0:T(4,128)S(1)}, u32[]{:S(2)}, u32[]{:S(2)}) collective-permute-start(f32[4,2048]{1,0:T(4,128)S(1)} %fusion.9), channel_id=1, source_target_pairs={{0,1},{1,4},{4,5},{5,8},{8,9},{9,12},{12,13},{2,3},{3,6},{6,7},{7,... | collective-permute-start | bytes 98312 | tf_op jit(solution)/shard_map/ppermute | solution.py:103
  74.4 6.7 %collective-permute-start.8 = (f32[4,2048]{1,0:T(4,128)S(1)}, f32[4,2048]{1,0:T(4,128)S(1)}, u32[]{:S(2)}, u32[]{:S(2)}) collective-permute-start(f32[4,2048]{1,0:T(4,128)S(1)} %add.102), channel_id=1, source_target_pairs={{0,4},{1,5},{4,8},{5,9},{8,12},{9,13},{2,6},{3,7},{6,10},{7,11},{1... | collective-permute-start | bytes 98312 | tf_op jit(solution)/shard_map/ppermute | solution.py:103
  81.1 1.6 %collective-permute-done.8 = f32[4,2048]{1,0:T(4,128)S(1)} collective-permute-done((f32[4,2048]{1,0:T(4,128)S(1)}, f32[4,2048]{1,0:T(4,128)S(1)}, u32[]{:S(2)}, u32[]{:S(2)}) %collective-permute-start.8) | collective-permute-done | bytes 32800 | tf_op jit(solution)/shard_map/ppermute | solution.py:103
  82.7 5.8 %collective-permute-start.9 = (f32[4,2048]{1,0:T(4,128)S(1)}, f32[4,2048]{1,0:T(4,128)S(1)}, u32[]{:S(2)}, u32[]{:S(2)}) collective-permute-start(f32[4,2048]{1,0:T(4,128)S(1)} %add.104), channel_id=1, source_target_pairs={{0,8},{1,9},{4,12},{5,13},{2,10},{3,11},{6,14},{7,15},{16,24},{17,... | collective-permute-start | bytes 98312 | tf_op jit(solution)/shard_map/ppermute | solution.py:103
  88.4 1.6 %collective-permute-done.9 = f32[4,2048]{1,0:T(4,128)S(1)} collective-permute-done((f32[4,2048]{1,0:T(4,128)S(1)}, f32[4,2048]{1,0:T(4,128)S(1)}, u32[]{:S(2)}, u32[]{:S(2)}) %collective-permute-start.9) | collective-permute-done | bytes 32800 | tf_op jit(solution)/shard_map/ppermute | solution.py:103
  (56 shorter events, 12.9 us)
Async XLA Ops:
  0.0 11.6 %copy-start = (bf16[1000,320]{0,1:T(8,128)(2,1)S(1)}, bf16[1000,320]{0,1:T(8,128)(2,1)}, u32[]{:S(2)}) copy-start(bf16[1000,320]{0,1:T(8,128)(2,1)} %param.16) | copy-start | bytes 1920004
  1.0 20.3 %collective-permute-start = (bf16[4,3,2048]{2,1,0:T(4,128)(2,1)S(1)}, bf16[4,3,2048]{2,1,0:T(4,128)(2,1)S(1)}, u32[]{:S(2)}, u32[]{:S(2)}) collective-permute-start(bf16[4,3,2048]{2,1,0:T(4,128)(2,1)S(1)} %get-tuple-element.21), channel_id=1, source_target_pairs={{0,2},{1,3},{4,6},{5,7},{8,10},{9,11},{12,14},{13,15},{16,18},{17,... | collective-permute-start | bytes 147464 | tf_op jit(solution)/shard_map/ppermute | solution.py:17
  5.9 15.4 %collective-permute-start.1 = (bf16[4,3,2048]{2,1,0:T(4,128)(2,1)S(1)}, bf16[4,3,2048]{2,1,0:T(4,128)(2,1)S(1)}, u32[]{:S(2)}, u32[]{:S(2)}) collective-permute-start(bf16[4,3,2048]{2,1,0:T(4,128)(2,1)S(1)} %get-tuple-element.22), channel_id=1, source_target_pairs={{2,0},{3,1},{6,4},{7,5},{10,8},{11,9},{14,12},{15,13},{18,16},{19,... | collective-permute-start | bytes 147464 | tf_op jit(solution)/shard_map/ppermute | solution.py:20
  16.7 4.6 %copy-start.5 = (bf16[4,4,2048]{2,1,0:T(4,128)(2,1)S(1)}, bf16[4,4,2048]{2,1,0:T(4,128)(2,1)}, u32[]{:S(2)}) copy-start(bf16[4,4,2048]{2,1,0:T(4,128)(2,1)} %param.12) | copy-start | bytes 196612
  21.8 1.1 %copy-start.1 = (bf16[2880,64]{1,0:T(8,128)(2,1)S(1)}, bf16[2880,64]{1,0:T(8,128)(2,1)}, u32[]{:S(2)}) copy-start(bf16[2880,64]{1,0:T(8,128)(2,1)} %copy.16) | copy-start | bytes 1105924
  22.9 1.0 %copy-start.3 = (bf16[576,320]{1,0:T(8,128)(2,1)S(1)}, bf16[576,320]{1,0:T(8,128)(2,1)}, u32[]{:S(2)}) copy-start(bf16[576,320]{1,0:T(8,128)(2,1)} %copy.14) | copy-start | bytes 1105924
  33.0 2.3 %collective-permute-start.2 = (f32[2,4,2048]{2,1,0:T(4,128)S(1)}, f32[2,4,2048]{2,1,0:T(4,128)S(1)}, u32[]{:S(2)}, u32[]{:S(2)}) collective-permute-start(f32[2,4,2048]{2,1,0:T(4,128)S(1)} %pad_maximum_fusion.2), channel_id=1, source_target_pairs={{0,1},{1,4},{4,5},{5,8},{8,9},{9,12},{12,13},{2,3},{3,6},{6,7},{7,... | collective-permute-start | bytes 196616 | tf_op jit(solution)/shard_map/ppermute | solution.py:103
  35.3 8.3 %collective-permute-start.3 = (f32[4,2048]{1,0:T(4,128)S(1)}, f32[4,2048]{1,0:T(4,128)S(1)}, u32[]{:S(2)}, u32[]{:S(2)}) collective-permute-start(f32[4,2048]{1,0:T(4,128)S(1)} %fusion.13), channel_id=1, source_target_pairs={{0,4},{1,5},{4,8},{5,9},{8,12},{9,13},{2,6},{3,7},{6,10},{7,11},{1... | collective-permute-start | bytes 98312 | tf_op jit(solution)/shard_map/ppermute | solution.py:103
  43.6 6.8 %collective-permute-start.4 = (f32[4,2048]{1,0:T(4,128)S(1)}, f32[4,2048]{1,0:T(4,128)S(1)}, u32[]{:S(2)}, u32[]{:S(2)}) collective-permute-start(f32[4,2048]{1,0:T(4,128)S(1)} %add.96), channel_id=1, source_target_pairs={{0,8},{1,9},{4,12},{5,13},{2,10},{3,11},{6,14},{7,15},{16,24},{17,... | collective-permute-start | bytes 98312 | tf_op jit(solution)/shard_map/ppermute | solution.py:103
  51.5 6.4 %collective-permute-start.5 = (bf16[4,3,2048]{2,1,0:T(4,128)(2,1)S(1)}, bf16[4,3,2048]{2,1,0:T(4,128)(2,1)S(1)}, u32[]{:S(2)}, u32[]{:S(2)}) collective-permute-start(bf16[4,3,2048]{2,1,0:T(4,128)(2,1)S(1)} %get-tuple-element.19), channel_id=1, source_target_pairs={{0,2},{1,3},{4,6},{5,7},{8,10},{9,11},{12,14},{13,15},{16,18},{17,... | collective-permute-start | bytes 147464 | tf_op jit(solution)/shard_map/ppermute | solution.py:17
  56.0 6.2 %collective-permute-start.6 = (bf16[4,3,2048]{2,1,0:T(4,128)(2,1)S(1)}, bf16[4,3,2048]{2,1,0:T(4,128)(2,1)S(1)}, u32[]{:S(2)}, u32[]{:S(2)}) collective-permute-start(bf16[4,3,2048]{2,1,0:T(4,128)(2,1)S(1)} %get-tuple-element.20), channel_id=1, source_target_pairs={{2,0},{3,1},{6,4},{7,5},{10,8},{11,9},{14,12},{15,13},{18,16},{19,... | collective-permute-start | bytes 147464 | tf_op jit(solution)/shard_map/ppermute | solution.py:20
  62.7 1.1 %copy-start.2 = (bf16[2880,64]{1,0:T(8,128)(2,1)S(1)}, bf16[2880,64]{1,0:T(8,128)(2,1)}, u32[]{:S(2)}) copy-start(bf16[2880,64]{1,0:T(8,128)(2,1)} %copy.16) | copy-start | bytes 1105924
  63.8 1.0 %copy-start.4 = (bf16[576,320]{1,0:T(8,128)(2,1)S(1)}, bf16[576,320]{1,0:T(8,128)(2,1)}, u32[]{:S(2)}) copy-start(bf16[576,320]{1,0:T(8,128)(2,1)} %copy.14) | copy-start | bytes 1105924
  64.8 25.2 %copy-start.6 = (f32[4,2048]{1,0:T(4,128)S(1)}, f32[4,2048]{1,0:T(4,128)}, u32[]{:S(2)}) copy-start(f32[4,2048]{1,0:T(4,128)} %param.11) | copy-start | bytes 98308
  72.2 2.1 %collective-permute-start.7 = (f32[4,2048]{1,0:T(4,128)S(1)}, f32[4,2048]{1,0:T(4,128)S(1)}, u32[]{:S(2)}, u32[]{:S(2)}) collective-permute-start(f32[4,2048]{1,0:T(4,128)S(1)} %fusion.9), channel_id=1, source_target_pairs={{0,1},{1,4},{4,5},{5,8},{8,9},{9,12},{12,13},{2,3},{3,6},{6,7},{7,... | collective-permute-start | bytes 98312 | tf_op jit(solution)/shard_map/ppermute | solution.py:103
  74.4 8.3 %collective-permute-start.8 = (f32[4,2048]{1,0:T(4,128)S(1)}, f32[4,2048]{1,0:T(4,128)S(1)}, u32[]{:S(2)}, u32[]{:S(2)}) collective-permute-start(f32[4,2048]{1,0:T(4,128)S(1)} %add.102), channel_id=1, source_target_pairs={{0,4},{1,5},{4,8},{5,9},{8,12},{9,13},{2,6},{3,7},{6,10},{7,11},{1... | collective-permute-start | bytes 98312 | tf_op jit(solution)/shard_map/ppermute | solution.py:103
  82.7 7.4 %collective-permute-start.9 = (f32[4,2048]{1,0:T(4,128)S(1)}, f32[4,2048]{1,0:T(4,128)S(1)}, u32[]{:S(2)}, u32[]{:S(2)}) collective-permute-start(f32[4,2048]{1,0:T(4,128)S(1)} %add.104), channel_id=1, source_target_pairs={{0,8},{1,9},{4,12},{5,13},{2,10},{3,11},{6,14},{7,15},{16,24},{17,... | collective-permute-start | bytes 98312 | tf_op jit(solution)/shard_map/ppermute | solution.py:103
